TPU v7x, 512 devices: a whole 4x8x8 slice. The times are simulated.
512 devices in a mesh: grp: 16 (over x, z_lo), ep: 32 (over y, z_hi, core).
Axes of the slice: x: 4, y: 8, z: 8 (z_hi: 2, z_lo: 4; z = z_hi * 4 + z_lo), core: 2. Of those that a mesh axis runs over, the one named last changes fastest.
Arguments:
- slot_hidden: bfloat16 [65536, 8, 768], P(('grp', 'ep')), may hold values from -6 to 6
- expert_ids: int32 [65536, 8], P(('grp', 'ep')), may hold values from 0 to 63, all different within a row; in each aligned block of 128 rows (0 to 127, 128 to 255, ...) at most 24 rows name the same one
- gate_fixed: int32 [65536, 8], P(('grp', 'ep')), may hold values from 1 to 65535
- master: float32 [64, 768, 2048], P('ep', 'grp'), may hold values from -6 to 6
- moment_one: bfloat16 [64, 768, 2048], P('ep', 'grp'), may hold values from -3 to 3
- moment_two: bfloat16 [64, 768, 2048], P('ep', 'grp'), may hold values from 0.0099487305 to 2
- gradient: bfloat16 [64, 768, 2048], P('ep', 'grp'), may hold values from -6 to 6
Outputs:
- mixed: bfloat16 [65536, 2048], P(('grp', 'ep'))
- backup: float32 [64, 768, 2048], P('ep', 'grp')
Inputs may be any that keep to these rules, and one draw needn't show every extreme that they name: `expert_ids`: in each aligned block of 128 rows (the rows of one device) no expert is named by more than 24 rows, a bound that some block reaches; the 8 experts of a row differ.
All inputs are finite; a program needn't handle non-finite values.
Results may differ from a plain program's by a relative error of at most 0.0057.
Values may be sent and summed in bfloat16 or wider, within the bound.
No kernel may reach another device: no remote copies, remote signals or barrier semaphores. Data moves between devices by JAX's collectives and lax.ppermute only.
A program may use at most 64 MiB of HBM per device.

v0:
```python
import math
import jax
import jax.numpy as jnp
from jax import lax
from jax.sharding import Mesh
from jax.sharding import PartitionSpec as P

GRP = ("grp_0", "grp_1")
GRP_EP = ("grp_0", "grp_1", "ep")
beta_one = 0.9
beta_two = 0.95
corr_one = 1.0 - 0.9**40
corr_two = 1.0 - 0.95**40
learn_rate = 0.05
decay_rate = 0.1
adam_eps = 1e-08
gate_unit = 65536.0


def from_behind(value, axis, steps):
    count = lax.axis_size(axis)
    pairs = [(source, (source + steps) % count) for source in range(count)]
    return lax.ppermute(value, axis, pairs)


def gather_axes(shard, axes, dim):
    if not axes:
        return shard
    nearer = lax.all_gather(shard, axes[-1], axis=dim, tiled=True)
    return gather_axes(nearer, axes[:-1], dim)


def cut_along(shard, dim, peers):
    dims = shard.shape
    tiles = shard.reshape(*dims[:dim], peers, dims[dim] // peers, *dims[dim + 1 :])
    return jnp.moveaxis(tiles, dim, 0)


def cut_rows(length, count):
    unit = 8 if length >= 8 * count else 1
    return [length // unit * k // count * unit for k in range(1, count)]


def laid_out(tiles, dim):
    dims = list(tiles.shape[1:])
    dims[dim] *= tiles.shape[0]
    return jnp.moveaxis(tiles, 0, dim).reshape(dims)


def exchange_in_pieces(shard, axis, pieces, split_dim, concat_dim):
    tiles = cut_along(shard, split_dim, lax.axis_size(axis))
    split_at = max(range(1, max(2, tiles.ndim - 1)), key=lambda d: tiles.shape[d])
    gathered = []
    for piece in jnp.split(tiles, cut_rows(tiles.shape[split_at], pieces), axis=split_at):
        if piece.size:
            gathered.append(lax.all_to_all(piece, axis, split_axis=0, concat_axis=0, tiled=True))
    return laid_out(jnp.concatenate(gathered, axis=split_at), concat_dim)


def adamw_step(master, moment_one, moment_two, gradient):
    widened = gradient.astype(jnp.float32)
    first_moment = beta_one * moment_one.astype(jnp.float32) + (1.0 - beta_one) * widened
    second_moment = beta_two * moment_two.astype(jnp.float32) + (1.0 - beta_two) * widened * widened
    return (
        first_moment / corr_one / (jnp.sqrt(second_moment / corr_two) + adam_eps)
        + decay_rate * master
    )


def slot_positions(ids_block, experts, capacity):
    onehot = (ids_block[:, None] == jnp.arange(experts, dtype=jnp.int32)[None, :]).astype(jnp.int32)
    before = jnp.cumsum(onehot, axis=0) - onehot
    slot_index = jnp.sum(before * onehot, axis=1)
    return ids_block * capacity + slot_index


def body(slot_hidden, expert_ids, gate_fixed, master, moment_one, moment_two, gradient):
    groups = lax.axis_size(GRP)
    ranks = lax.axis_size("ep")
    local_experts = master.shape[0]
    experts = local_experts * ranks
    tok_count, top_count, hidden_width = slot_hidden.shape
    width = master.shape[2]
    capacity = max(2, tok_count * top_count // experts + tok_count * top_count // (2 * experts))
    scaling = 1.0 / math.sqrt(hidden_width)
    step_dir = adamw_step(master, moment_one, moment_two, gradient)
    updated = master - learn_rate * step_dir
    partner_master = from_behind(master.astype(jnp.bfloat16), GRP, groups // 2).astype(master.dtype)
    partner_rest = from_behind((moment_one, moment_two, gradient), GRP, groups // 2)
    backup = adamw_step(partner_master, partner_rest[0], partner_rest[1], partner_rest[2])
    weights = updated.astype(jnp.bfloat16)
    pairs = tok_count * top_count
    positions = slot_positions(expert_ids.reshape(pairs), experts, capacity)
    outgoing = jnp.zeros((experts * capacity, hidden_width), jnp.bfloat16)
    outgoing = outgoing.at[positions].set(slot_hidden.reshape(pairs, hidden_width))
    outgoing = outgoing.reshape(experts, capacity, hidden_width)
    arrived = lax.all_to_all(outgoing, "ep", split_axis=0, concat_axis=1, tiled=True)
    gathered = gather_axes(weights, GRP, 1)
    product = jnp.einsum("erh,ehd->erd", arrived, gathered, preferred_element_type=jnp.float32)
    results = (product * scaling).astype(jnp.bfloat16)
    returned = exchange_in_pieces(results, "ep", 2, 1, 0)
    picked = returned.reshape(experts * capacity, width)[positions]
    factors = gate_fixed.reshape(pairs).astype(jnp.float32) / gate_unit
    weighted = (picked.astype(jnp.float32) * factors[:, None]).reshape(tok_count, top_count, width)
    mixed = jnp.sum(weighted, axis=1).astype(jnp.bfloat16)
    return (mixed, backup)


def solution(mesh):
    torus = Mesh(mesh.devices.reshape(4, 4, mesh.shape["ep"]), ("grp_0", "grp_1", "ep"))
    in_specs = (
        P(GRP_EP, None, None),
        P(GRP_EP, None),
        P(GRP_EP, None),
        P("ep", GRP, None),
        P("ep", GRP, None),
        P("ep", GRP, None),
        P("ep", GRP, None),
    )
    out_specs = (P(GRP_EP, None), P("ep", GRP, None))
    return jax.shard_map(body, mesh=torus, in_specs=in_specs, out_specs=out_specs, check_vma=False)
```

profile of v0, /device:TPU:21, one launch (start us, length us, event | category | flops | bytes accessed | tf_op | source)
XLA Modules:
  0.0 392.5 jit_solution(8593457974764892059)
XLA Ops:
  7.2 3.4 fusion.27
  10.7 49.0 %all-gather.3.cloned.1.call-done = bf16[2,192,2048]{2,1,0:T(8,128)(2,1)} async-done(((bf16[2,48,2048]{2,1,0:T(8,128)(2,1)}), bf16[2,192,2048]{2,1,0:T(8,128)(2,1)}) %all-gather.3.cloned.1.call-update) | async-done | bytes 1572880 | tf_op jit(solution)/shard_map/all_gather | solution.py:29
  60.1 18.0 %reduce-window.6 = s32[64,8,128]{2,1,0:T(8,128)S(1)} reduce-window(s32[64,8,128]{2,1,0:T(8,128)S(1)} %fusion.26, s32[]{:T(128)} %constant.8.clone.1), window={size=1x1x128 pad=0_0x0_0x127_0}, to_apply=%region_0.0 | reduce-window | flops 8323072 | bytes 524292 | tf_op jit(solution)/shard_map/reduce-window
  78.9 6.9 %scatter_custom_fusion = bf16[1536,768]{1,0:T(8,128)(2,1)} fusion(s32[1024]{0:T(1024)S(1)} %bitcast.48, bf16[128,8,768]{2,1,0:T(8,128)(2,1)S(1)} %copy-done, bf16[]{:T(256)} %constant.14.clone.1), kind=kCustom, calls=%fused_computation.7 | custom fusion | bytes 3932162 | tf_op jit(solution)/shard_map/scatter | solution.py:95
  85.9 70.6 %all_to_all.28 = bf16[64,24,768]{2,1,0:T(8,128)(2,1)S(1)} all-to-all(bf16[64,24,768]{2,1,0:T(8,128)(2,1)} %bitcast.41), channel_id=1, replica_groups=mesh['grp_0'=4,'grp_1'=4,'ep'=32] {'ep'}, dimensions={0} | all-to-all | bytes 4718592 | tf_op jit(solution)/shard_map/all_to_all | solution.py:97
  156.4 1.6 copy.24
  158.0 7.9 %multiply_convert_fusion = bf16[2,768,2048]{2,1,0:T(8,128)(2,1)S(1)} fusion(bf16[2,768,768]{2,1,0:T(8,128)(2,1)} %bitcast.44, bf16[2,768,2048]{2,1,0:T(8,128)(2,1)} %all-gather.5.cloned.1.call-done), kind=kOutput, calls=%fused_computation.2 | convolution fusion | flops 4838129664 | bytes 14942208 | tf_op jit(solution)/shard_map/erh,ehd->erd/dot_general | solution.py:99
  165.9 1.1 copy.30
  167.0 2.7 copy-done.1
  169.7 1.5 split.8
  171.2 6.9 %all-to-all-start.1 = ((bf16[32,2,8,2048]{3,2,1,0:T(8,128)(2,1)}), bf16[32,2,8,2048]{3,2,1,0:T(8,128)(2,1)}, u32[]{:S(2)}, u32[]{:S(2)}) async-start(bf16[32,2,8,2048]{3,2,1,0:T(8,128)(2,1)} %split.8), calls=%async_computation.1 | async-start | bytes 4194304 | tf_op jit(solution)/shard_map/all_to_all | solution.py:56
  178.1 4.8 %split.9 = bf16[32,2,16,2048]{3,2,1,0:T(8,128)(2,1)} slice(bf16[32,2,24,2048]{3,2,1,0:T(8,128)(2,1)} %bitcast.40), slice={[0:32], [0:2], [8:24], [0:2048]} | slice | bytes 8388608 | tf_op jit(solution)/shard_map/split | solution.py:54
  183.0 45.7 %all-to-all-done.1 = bf16[32,2,8,2048]{3,2,1,0:T(8,128)(2,1)} async-done(((bf16[32,2,8,2048]{3,2,1,0:T(8,128)(2,1)}), bf16[32,2,8,2048]{3,2,1,0:T(8,128)(2,1)}, u32[]{:S(2)}, u32[]{:S(2)}) %all-to-all-start.1) | async-done | bytes 2097184 | tf_op jit(solution)/shard_map/all_to_all | solution.py:56
  228.6 14.3 %all-to-all-start.2 = ((bf16[32,2,16,2048]{3,2,1,0:T(8,128)(2,1)}), bf16[32,2,16,2048]{3,2,1,0:T(8,128)(2,1)}, u32[]{:S(2)}, u32[]{:S(2)}) async-start(bf16[32,2,16,2048]{3,2,1,0:T(8,128)(2,1)} %split.9), calls=%async_computation.2 | async-start | bytes 8388608 | tf_op jit(solution)/shard_map/all_to_all | solution.py:56
  242.9 1.9 collective-permute-start
  244.9 4.9 %collective-permute-start.1 = (bf16[2,48,2048]{2,1,0:T(8,128)(2,1)}, bf16[2,48,2048]{2,1,0:T(8,128)(2,1)S(1)}, u32[]{:S(2)}, u32[]{:S(2)}) collective-permute-start(bf16[2,48,2048]{2,1,0:T(8,128)(2,1)} %param.13), channel_id=1, source_target_pairs={{0,256},{32,288},{64,320},{96,352},{128,384},{160,416},{192,448},{... | collective-permute-start | bytes 1179656 | tf_op jit(solution)/shard_map/ppermute | solution.py:23
  249.8 1.9 collective-permute-start.2
  251.7 5.0 %collective-permute-start.3 = (bf16[2,48,2048]{2,1,0:T(8,128)(2,1)}, bf16[2,48,2048]{2,1,0:T(8,128)(2,1)S(1)}, u32[]{:S(2)}, u32[]{:S(2)}) collective-permute-start(bf16[2,48,2048]{2,1,0:T(8,128)(2,1)} %get-tuple-element.2), channel_id=1, source_target_pairs={{0,256},{32,288},{64,320},{96,352},{128,384},{160,416},{192,448},{... | collective-permute-start | bytes 1179656 | tf_op jit(solution)/shard_map/ppermute | solution.py:23
  257.5 24.6 %collective-permute-done.3 = bf16[2,48,2048]{2,1,0:T(8,128)(2,1)S(1)} collective-permute-done((bf16[2,48,2048]{2,1,0:T(8,128)(2,1)}, bf16[2,48,2048]{2,1,0:T(8,128)(2,1)S(1)}, u32[]{:S(2)}, u32[]{:S(2)}) %collective-permute-start.3) | collective-permute-done | bytes 393248 | tf_op jit(solution)/shard_map/ppermute | solution.py:23
  282.1 1.5 fusion.13
  283.6 75.7 %all-to-all-done.2 = bf16[32,2,16,2048]{3,2,1,0:T(8,128)(2,1)} async-done(((bf16[32,2,16,2048]{3,2,1,0:T(8,128)(2,1)}), bf16[32,2,16,2048]{3,2,1,0:T(8,128)(2,1)}, u32[]{:S(2)}, u32[]{:S(2)}) %all-to-all-start.2) | async-done | bytes 4194336 | tf_op jit(solution)/shard_map/all_to_all | solution.py:56
  359.3 6.7 %pad_maximum_fusion = bf16[32,2,24,2048]{3,2,1,0:T(8,128)(2,1)} fusion(bf16[32,2,16,2048]{3,2,1,0:T(8,128)(2,1)} %all-to-all-done.2, bf16[32,2,8,2048]{3,2,1,0:T(8,128)(2,1)} %all-to-all-done.1), kind=kLoop, calls=%fused_computation.5 | loop fusion | flops 12582912 | bytes 12582912 | tf_op jit(solution)/shard_map/concatenate | solution.py:57
  366.0 12.4 %gather_fusion = bf16[1024,2048]{1,0:T(8,128)(2,1)} fusion(bf16[1536,2048]{1,0:T(8,128)(2,1)} %bitcast.38, s32[1024]{0:T(1024)S(1)} %broadcast_clamp_fusion), kind=kCustom, calls=%fused_computation | custom fusion | bytes 8392704 | tf_op jit(solution)/shard_map/gather | solution.py:102
  378.4 7.3 %fusion = bf16[128,2048]{1,0:T(8,128)(2,1)} fusion(bf16[1024,2048]{1,0:T(8,128)(2,1)} %gather_fusion, f32[128,8]{1,0:T(8,128)S(1)} %copy-done.3), kind=kLoop, calls=%fused_computation.4 | loop fusion | flops 6029312 | bytes 4722688 | tf_op jit(solution)/shard_map/reduce_sum | solution.py:105
  (37 shorter events, 2.0 us)
Async XLA Ops:
  7.2 71.8 %copy-start = (bf16[128,8,768]{2,1,0:T(8,128)(2,1)S(1)}, bf16[128,8,768]{2,1,0:T(8,128)(2,1)}, u32[]{:S(2)}) copy-start(bf16[128,8,768]{2,1,0:T(8,128)(2,1)} %param.7) | copy-start | bytes 4718596
  7.2 52.6 %copy-start.4 = (s32[128,8]{0,1:T(8,128)S(1)}, s32[128,8]{0,1:T(8,128)}, u32[]{:S(2)}) copy-start(s32[128,8]{0,1:T(8,128)} %param.8) | copy-start | bytes 12292
  7.2 52.5 %all-gather.3.cloned.1.call-start = ((), (), s32[]{:S(2)}) async-start(), calls=%async_computation.3 | async-start | bytes 1966080 | tf_op jit(solution)/shard_map/all_gather | solution.py:29
  10.6 147.4 %all-gather.5.cloned.1.call-start = ((), (), s32[]{:S(2)}) async-start(), calls=%async_computation.4 | async-start | bytes 7864320 | tf_op jit(solution)/shard_map/all_gather | solution.py:29
  167.0 2.7 copy-start.1
  171.2 57.4 %all-to-all-start.1 = ((bf16[32,2,8,2048]{3,2,1,0:T(8,128)(2,1)}), bf16[32,2,8,2048]{3,2,1,0:T(8,128)(2,1)}, u32[]{:S(2)}, u32[]{:S(2)}) async-start(bf16[32,2,8,2048]{3,2,1,0:T(8,128)(2,1)} %split.8), calls=%async_computation.1 | async-start | bytes 4194304 | tf_op jit(solution)/shard_map/all_to_all | solution.py:56
  182.9 60.0 %copy-start.2 = (bf16[2,48,2048]{2,1,0:T(8,128)(2,1)S(1)}, bf16[2,48,2048]{2,1,0:T(8,128)(2,1)}, u32[]{:S(2)}) copy-start(bf16[2,48,2048]{2,1,0:T(8,128)(2,1)} %param.11) | copy-start | bytes 1179652
  183.0 73.8 %copy-start.5 = (s32[128,8]{0,1:T(8,128)S(1)}, s32[128,8]{0,1:T(8,128)}, u32[]{:S(2)}) copy-start(s32[128,8]{0,1:T(8,128)} %param.9) | copy-start | bytes 12292
  228.6 130.7 %all-to-all-start.2 = ((bf16[32,2,16,2048]{3,2,1,0:T(8,128)(2,1)}), bf16[32,2,16,2048]{3,2,1,0:T(8,128)(2,1)}, u32[]{:S(2)}, u32[]{:S(2)}) async-start(bf16[32,2,16,2048]{3,2,1,0:T(8,128)(2,1)} %split.9), calls=%async_computation.2 | async-start | bytes 8388608 | tf_op jit(solution)/shard_map/all_to_all | solution.py:56
  242.9 39.1 %collective-permute-start = (bf16[2,48,2048]{2,1,0:T(8,128)(2,1)S(1)}, bf16[2,48,2048]{2,1,0:T(8,128)(2,1)S(1)}, u32[]{:S(2)}, u32[]{:S(2)}) collective-permute-start(bf16[2,48,2048]{2,1,0:T(8,128)(2,1)S(1)} %copy-done.2), channel_id=1, source_target_pairs={{0,256},{32,288},{64,320},{96,352},{128,384},{160,416},{192,448},{... | collective-permute-start | bytes 1179656 | tf_op jit(solution)/shard_map/ppermute | solution.py:23
  244.9 37.2 %collective-permute-start.1 = (bf16[2,48,2048]{2,1,0:T(8,128)(2,1)}, bf16[2,48,2048]{2,1,0:T(8,128)(2,1)S(1)}, u32[]{:S(2)}, u32[]{:S(2)}) collective-permute-start(bf16[2,48,2048]{2,1,0:T(8,128)(2,1)} %param.13), channel_id=1, source_target_pairs={{0,256},{32,288},{64,320},{96,352},{128,384},{160,416},{192,448},{... | collective-permute-start | bytes 1179656 | tf_op jit(solution)/shard_map/ppermute | solution.py:23
  249.8 32.3 %collective-permute-start.2 = (bf16[2,48,2048]{2,1,0:T(8,128)(2,1)}, bf16[2,48,2048]{2,1,0:T(8,128)(2,1)S(1)}, u32[]{:S(2)}, u32[]{:S(2)}) collective-permute-start(bf16[2,48,2048]{2,1,0:T(8,128)(2,1)} %param.12), channel_id=1, source_target_pairs={{0,256},{32,288},{64,320},{96,352},{128,384},{160,416},{192,448},{... | collective-permute-start | bytes 1179656 | tf_op jit(solution)/shard_map/ppermute | solution.py:23
  251.7 30.4 %collective-permute-start.3 = (bf16[2,48,2048]{2,1,0:T(8,128)(2,1)}, bf16[2,48,2048]{2,1,0:T(8,128)(2,1)S(1)}, u32[]{:S(2)}, u32[]{:S(2)}) collective-permute-start(bf16[2,48,2048]{2,1,0:T(8,128)(2,1)} %get-tuple-element.2), channel_id=1, source_target_pairs={{0,256},{32,288},{64,320},{96,352},{128,384},{160,416},{192,448},{... | collective-permute-start | bytes 1179656 | tf_op jit(solution)/shard_map/ppermute | solution.py:23
  366.0 12.4 %copy-start.3 = (f32[128,8]{1,0:T(8,128)S(1)}, f32[128,8]{1,0:T(8,128)}, u32[]{:S(2)}) copy-start(f32[128,8]{1,0:T(8,128)} %copy.26) | copy-start | bytes 12292
Sparse Core Ops, SparseCore 0:
  10.7 48.9 all-gather.2
  61.8 69.9 all-gather.4
where the time goes:
time: 393 us
  waiting for transfers between devices  195 us (50%)
  blocking collectives  70.6 us (18%)
  other arithmetic  37.1 us (9%)
  starting transfers between devices  35.1 us (9%)
  local copies, waits for them, and re-layouts  32.7 us (8%)
  between operations  14.2 us (4%)
  matrix products  7.85 us (2%)
    all_to_all x2, waiting for transfers between devices, exchange_in_pieces(): lax.all_to_all(piece, axis, split_axis=0, concat_axis=0, tiled=True)  121 us
    all_to_all x1, blocking collectives, body(): lax.all_to_all(outgoing, 'ep', split_axis=0, concat_axis=1, tiled=True)  70.6 us
    all_gather x2, waiting for transfers between devices, gather_axes(): nearer = lax.all_gather(shard, axes[-1], axis=dim, tiled=True)  49 us
    ppermute x4, waiting for transfers between devices, from_behind(): return lax.ppermute(value, axis, pairs)  24.6 us
    all_to_all x2, starting transfers between devices, exchange_in_pieces(): lax.all_to_all(piece, axis, split_axis=0, concat_axis=0, tiled=True)  21.2 us
    another operation x3, other arithmetic  18.2 us
    ppermute x4, starting transfers between devices, from_behind(): return lax.ppermute(value, axis, pairs)  13.8 us
    gather x1, local copies, waits for them, and re-layouts, body(): picked = returned.reshape(experts * capacity, width)[positions]  12.4 us
  transfers between devices with their start and end apart: 8, of which 4 were waited for; matrix products, arithmetic and copies ran while one was open for 9% of the time, Pallas kernels for 0%

commit v1 on v0

--- a/solution.py
+++ b/solution.py
@@ -15,6 +15,12 @@
 decay_rate = 0.1
 adam_eps = 1e-08
 gate_unit = 65536.0
+
+
+def trade_parts(shard, axis, split, join):
+    parts = jnp.split(shard, lax.axis_size(axis), axis=split)
+    arrived = lax.all_to_all(jnp.stack(parts), axis, 0, 0)
+    return jnp.concatenate(arrived, axis=join)
 
 
 def from_behind(value, axis, steps):
@@ -94,7 +100,7 @@
     outgoing = jnp.zeros((experts * capacity, hidden_width), jnp.bfloat16)
     outgoing = outgoing.at[positions].set(slot_hidden.reshape(pairs, hidden_width))
     outgoing = outgoing.reshape(experts, capacity, hidden_width)
-    arrived = lax.all_to_all(outgoing, "ep", split_axis=0, concat_axis=1, tiled=True)
+    arrived = trade_parts(outgoing, "ep", 0, 1)
     gathered = gather_axes(weights, GRP, 1)
     product = jnp.einsum("erh,ehd->erd", arrived, gathered, preferred_element_type=jnp.float32)
     results = (product * scaling).astype(jnp.bfloat16)

time: 393 us -> 376 us (0.957)
  the two profiles are of different devices: /device:TPU:21 before, /device:TPU:19 now
where the time goes in v1:
time: 376 us
  waiting for transfers between devices  177 us (47%)
  blocking collectives  70.3 us (19%)
  other arithmetic  37.1 us (10%)
  local copies, waits for them, and re-layouts  34.9 us (9%)
  starting transfers between devices  33.8 us (9%)
  between operations  14.5 us (4%)
  matrix products  7.85 us (2%)
    all_to_all x2, waiting for transfers between devices, exchange_in_pieces(): lax.all_to_all(piece, axis, split_axis=0, concat_axis=0, tiled=True)  122 us
    all_to_all x1, blocking collectives, trade_parts(): arrived = lax.all_to_all(jnp.stack(parts), axis, 0, 0)  70.3 us
    all_gather x2, waiting for transfers between devices, gather_axes(): nearer = lax.all_gather(shard, axes[-1], axis=dim, tiled=True)  30.4 us
    ppermute x4, waiting for transfers between devices, from_behind(): return lax.ppermute(value, axis, pairs)  24.6 us
    all_to_all x2, starting transfers between devices, exchange_in_pieces(): lax.all_to_all(piece, axis, split_axis=0, concat_axis=0, tiled=True)  19.9 us
    another operation x3, other arithmetic  18.2 us
    ppermute x4, starting transfers between devices, from_behind(): return lax.ppermute(value, axis, pairs)  13.8 us
    gather x1, local copies, waits for them, and re-layouts, body(): picked = returned.reshape(experts * capacity, width)[positions]  12.4 us
  transfers between devices with their start and end apart: 8, of which 4 were waited for; matrix products, arithmetic and copies ran while one was open for 10% of the time, Pallas kernels for 0%

profile of v1, /device:TPU:19, one launch (start us, length us, event | category | flops | bytes accessed | tf_op | source)
XLA Modules:
  0.0 375.7 jit_solution(15724488908924166134)
XLA Ops:
  7.2 3.4 fusion.29
  11.0 18.0 %reduce-window.6 = s32[64,8,128]{2,1,0:T(8,128)S(1)} reduce-window(s32[64,8,128]{2,1,0:T(8,128)S(1)} %fusion.26, s32[]{:T(128)} %constant.8.clone.1), window={size=1x1x128 pad=0_0x0_0x127_0}, to_apply=%region_0.0 | reduce-window | flops 8323072 | bytes 524292 | tf_op jit(solution)/shard_map/reduce-window
  29.4 30.4 %all-gather.3.cloned.1.call-done = bf16[2,192,2048]{2,1,0:T(8,128)(2,1)} async-done(((bf16[2,48,2048]{2,1,0:T(8,128)(2,1)}), bf16[2,192,2048]{2,1,0:T(8,128)(2,1)}) %all-gather.3.cloned.1.call-update) | async-done | bytes 1572880 | tf_op jit(solution)/shard_map/all_gather | solution.py:35
  60.3 7.0 %scatter_custom_fusion = bf16[1536,768]{1,0:T(8,128)(2,1)} fusion(s32[1024]{0:T(1024)S(1)} %bitcast.108, bf16[128,8,768]{2,1,0:T(8,128)(2,1)S(1)} %copy-done, bf16[]{:T(256)} %constant.14.clone.1), kind=kCustom, calls=%fused_computation.7 | custom fusion | bytes 3932162 | tf_op jit(solution)/shard_map/scatter | solution.py:101
  67.2 1.5 fusion.28
  69.7 70.3 %all_to_all.15 = bf16[32,2,24,768]{3,2,1,0:T(8,128)(2,1)S(1)} all-to-all(bf16[32,2,24,768]{3,2,1,0:T(8,128)(2,1)S(1)} %constant_dynamic-update-slice_fusion), channel_id=1, replica_groups=mesh['grp_0'=4,'grp_1'=4,'ep'=32] {'ep'}, dimensions={0} | all-to-all | bytes 4718592 | tf_op jit(solution)/shard_map/all_to_all | solution.py:22
  140.0 1.6 copy.23
  141.6 7.9 %multiply_convert_fusion = bf16[2,768,2048]{2,1,0:T(8,128)(2,1)S(1)} fusion(bf16[2,768,768]{2,1,0:T(8,128)(2,1)} %bitcast.72, bf16[2,768,2048]{2,1,0:T(8,128)(2,1)} %all-gather.5.cloned.1.call-done), kind=kOutput, calls=%fused_computation.2 | convolution fusion | flops 4838129664 | bytes 14942208 | tf_op jit(solution)/shard_map/erh,ehd->erd/dot_general | solution.py:105
  150.6 2.7 copy-done.1
  153.3 1.5 split.168
  154.8 7.0 %all-to-all-start.1 = ((bf16[32,2,8,2048]{3,2,1,0:T(8,128)(2,1)}), bf16[32,2,8,2048]{3,2,1,0:T(8,128)(2,1)}, u32[]{:S(2)}, u32[]{:S(2)}) async-start(bf16[32,2,8,2048]{3,2,1,0:T(8,128)(2,1)} %split.168), calls=%async_computation.1 | async-start | bytes 4194304 | tf_op jit(solution)/shard_map/all_to_all | solution.py:62
  161.8 4.9 %split.169 = bf16[32,2,16,2048]{3,2,1,0:T(8,128)(2,1)} slice(bf16[32,2,24,2048]{3,2,1,0:T(8,128)(2,1)} %bitcast.69), slice={[0:32], [0:2], [8:24], [0:2048]} | slice | bytes 8388608 | tf_op jit(solution)/shard_map/split | solution.py:60
  166.7 45.8 %all-to-all-done.1 = bf16[32,2,8,2048]{3,2,1,0:T(8,128)(2,1)} async-done(((bf16[32,2,8,2048]{3,2,1,0:T(8,128)(2,1)}), bf16[32,2,8,2048]{3,2,1,0:T(8,128)(2,1)}, u32[]{:S(2)}, u32[]{:S(2)}) %all-to-all-start.1) | async-done | bytes 2097184 | tf_op jit(solution)/shard_map/all_to_all | solution.py:62
  212.4 12.9 %all-to-all-start.2 = ((bf16[32,2,16,2048]{3,2,1,0:T(8,128)(2,1)}), bf16[32,2,16,2048]{3,2,1,0:T(8,128)(2,1)}, u32[]{:S(2)}, u32[]{:S(2)}) async-start(bf16[32,2,16,2048]{3,2,1,0:T(8,128)(2,1)} %split.169), calls=%async_computation.2 | async-start | bytes 8388608 | tf_op jit(solution)/shard_map/all_to_all | solution.py:62
  225.3 3.8 %collective-permute-start = (bf16[2,48,2048]{2,1,0:T(8,128)(2,1)S(1)}, bf16[2,48,2048]{2,1,0:T(8,128)(2,1)S(1)}, u32[]{:S(2)}, u32[]{:S(2)}) collective-permute-start(bf16[2,48,2048]{2,1,0:T(8,128)(2,1)S(1)} %copy-done.3), channel_id=1, source_target_pairs={{0,256},{32,288},{64,320},{96,352},{128,384},{160,416},{192,448},{... | collective-permute-start | bytes 1179656 | tf_op jit(solution)/shard_map/ppermute | solution.py:29
  229.2 3.0 collective-permute-start.1
  232.2 3.8 %collective-permute-start.2 = (bf16[2,48,2048]{2,1,0:T(8,128)(2,1)}, bf16[2,48,2048]{2,1,0:T(8,128)(2,1)S(1)}, u32[]{:S(2)}, u32[]{:S(2)}) collective-permute-start(bf16[2,48,2048]{2,1,0:T(8,128)(2,1)} %param.12), channel_id=1, source_target_pairs={{0,256},{32,288},{64,320},{96,352},{128,384},{160,416},{192,448},{... | collective-permute-start | bytes 1179656 | tf_op jit(solution)/shard_map/ppermute | solution.py:29
  236.0 3.1 collective-permute-start.3
  239.9 24.6 %collective-permute-done.3 = bf16[2,48,2048]{2,1,0:T(8,128)(2,1)S(1)} collective-permute-done((bf16[2,48,2048]{2,1,0:T(8,128)(2,1)}, bf16[2,48,2048]{2,1,0:T(8,128)(2,1)S(1)}, u32[]{:S(2)}, u32[]{:S(2)}) %collective-permute-start.3) | collective-permute-done | bytes 393248 | tf_op jit(solution)/shard_map/ppermute | solution.py:29
  264.5 1.5 fusion.13
  266.0 76.4 %all-to-all-done.2 = bf16[32,2,16,2048]{3,2,1,0:T(8,128)(2,1)} async-done(((bf16[32,2,16,2048]{3,2,1,0:T(8,128)(2,1)}), bf16[32,2,16,2048]{3,2,1,0:T(8,128)(2,1)}, u32[]{:S(2)}, u32[]{:S(2)}) %all-to-all-start.2) | async-done | bytes 4194336 | tf_op jit(solution)/shard_map/all_to_all | solution.py:62
  342.4 6.7 %pad_maximum_fusion = bf16[32,2,24,2048]{3,2,1,0:T(8,128)(2,1)} fusion(bf16[32,2,16,2048]{3,2,1,0:T(8,128)(2,1)} %all-to-all-done.2, bf16[32,2,8,2048]{3,2,1,0:T(8,128)(2,1)} %all-to-all-done.1), kind=kLoop, calls=%fused_computation.5 | loop fusion | flops 12582912 | bytes 12582912 | tf_op jit(solution)/shard_map/concatenate | solution.py:63
  349.1 12.4 %gather_fusion = bf16[1024,2048]{1,0:T(8,128)(2,1)} fusion(bf16[1536,2048]{1,0:T(8,128)(2,1)} %bitcast.67, s32[1024]{0:T(1024)S(1)} %broadcast_clamp_fusion), kind=kCustom, calls=%fused_computation | custom fusion | bytes 8392704 | tf_op jit(solution)/shard_map/gather | solution.py:108
  361.5 7.3 %fusion = bf16[128,2048]{1,0:T(8,128)(2,1)} fusion(bf16[1024,2048]{1,0:T(8,128)(2,1)} %gather_fusion, f32[128,8]{1,0:T(8,128)S(1)} %copy-done.4), kind=kLoop, calls=%fused_computation.4 | loop fusion | flops 6029312 | bytes 4722688 | tf_op jit(solution)/shard_map/reduce_sum | solution.py:111
  (73 shorter events, 3.8 us)
Async XLA Ops:
  7.2 53.1 %copy-start = (bf16[128,8,768]{2,1,0:T(8,128)(2,1)S(1)}, bf16[128,8,768]{2,1,0:T(8,128)(2,1)}, u32[]{:S(2)}) copy-start(bf16[128,8,768]{2,1,0:T(8,128)(2,1)} %param.7) | copy-start | bytes 4718596
  7.2 3.5 copy-start.5
  7.2 52.6 %all-gather.3.cloned.1.call-start = ((), (), s32[]{:S(2)}) async-start(), calls=%async_computation.3 | async-start | bytes 1966080 | tf_op jit(solution)/shard_map/all_gather | solution.py:35
  10.6 131.0 %all-gather.5.cloned.1.call-start = ((), (), s32[]{:S(2)}) async-start(), calls=%async_computation.4 | async-start | bytes 7864320 | tf_op jit(solution)/shard_map/all_gather | solution.py:35
  67.2 2.1 copy-start.2
  150.6 2.7 copy-start.1
  154.8 57.6 %all-to-all-start.1 = ((bf16[32,2,8,2048]{3,2,1,0:T(8,128)(2,1)}), bf16[32,2,8,2048]{3,2,1,0:T(8,128)(2,1)}, u32[]{:S(2)}, u32[]{:S(2)}) async-start(bf16[32,2,8,2048]{3,2,1,0:T(8,128)(2,1)} %split.168), calls=%async_computation.1 | async-start | bytes 4194304 | tf_op jit(solution)/shard_map/all_to_all | solution.py:62
  166.6 58.7 %copy-start.3 = (bf16[2,48,2048]{2,1,0:T(8,128)(2,1)S(1)}, bf16[2,48,2048]{2,1,0:T(8,128)(2,1)}, u32[]{:S(2)}) copy-start(bf16[2,48,2048]{2,1,0:T(8,128)(2,1)} %param.11) | copy-start | bytes 1179652
  166.7 72.5 %copy-start.6 = (s32[128,8]{0,1:T(8,128)S(1)}, s32[128,8]{0,1:T(8,128)}, u32[]{:S(2)}) copy-start(s32[128,8]{0,1:T(8,128)} %param.9) | copy-start | bytes 12292
  212.4 130.0 %all-to-all-start.2 = ((bf16[32,2,16,2048]{3,2,1,0:T(8,128)(2,1)}), bf16[32,2,16,2048]{3,2,1,0:T(8,128)(2,1)}, u32[]{:S(2)}, u32[]{:S(2)}) async-start(bf16[32,2,16,2048]{3,2,1,0:T(8,128)(2,1)} %split.169), calls=%async_computation.2 | async-start | bytes 8388608 | tf_op jit(solution)/shard_map/all_to_all | solution.py:62
  225.3 39.1 %collective-permute-start = (bf16[2,48,2048]{2,1,0:T(8,128)(2,1)S(1)}, bf16[2,48,2048]{2,1,0:T(8,128)(2,1)S(1)}, u32[]{:S(2)}, u32[]{:S(2)}) collective-permute-start(bf16[2,48,2048]{2,1,0:T(8,128)(2,1)S(1)} %copy-done.3), channel_id=1, source_target_pairs={{0,256},{32,288},{64,320},{96,352},{128,384},{160,416},{192,448},{... | collective-permute-start | bytes 1179656 | tf_op jit(solution)/shard_map/ppermute | solution.py:29
  229.2 35.3 %collective-permute-start.1 = (bf16[2,48,2048]{2,1,0:T(8,128)(2,1)}, bf16[2,48,2048]{2,1,0:T(8,128)(2,1)S(1)}, u32[]{:S(2)}, u32[]{:S(2)}) collective-permute-start(bf16[2,48,2048]{2,1,0:T(8,128)(2,1)} %param.13), channel_id=1, source_target_pairs={{0,256},{32,288},{64,320},{96,352},{128,384},{160,416},{192,448},{... | collective-permute-start | bytes 1179656 | tf_op jit(solution)/shard_map/ppermute | solution.py:29
  232.2 32.3 %collective-permute-start.2 = (bf16[2,48,2048]{2,1,0:T(8,128)(2,1)}, bf16[2,48,2048]{2,1,0:T(8,128)(2,1)S(1)}, u32[]{:S(2)}, u32[]{:S(2)}) collective-permute-start(bf16[2,48,2048]{2,1,0:T(8,128)(2,1)} %param.12), channel_id=1, source_target_pairs={{0,256},{32,288},{64,320},{96,352},{128,384},{160,416},{192,448},{... | collective-permute-start | bytes 1179656 | tf_op jit(solution)/shard_map/ppermute | solution.py:29
  236.0 28.5 %collective-permute-start.3 = (bf16[2,48,2048]{2,1,0:T(8,128)(2,1)}, bf16[2,48,2048]{2,1,0:T(8,128)(2,1)S(1)}, u32[]{:S(2)}, u32[]{:S(2)}) collective-permute-start(bf16[2,48,2048]{2,1,0:T(8,128)(2,1)} %get-tuple-element.34), channel_id=1, source_target_pairs={{0,256},{32,288},{64,320},{96,352},{128,384},{160,416},{192,448},{... | collective-permute-start | bytes 1179656 | tf_op jit(solution)/shard_map/ppermute | solution.py:29
  349.1 12.4 %copy-start.4 = (f32[128,8]{1,0:T(8,128)S(1)}, f32[128,8]{1,0:T(8,128)}, u32[]{:S(2)}) copy-start(f32[128,8]{1,0:T(8,128)} %copy.25) | copy-start | bytes 12292
Sparse Core Ops, SparseCore 0:
  10.7 49.0 all-gather.2
  61.9 70.1 all-gather.4
